TPU v7x, 256 devices: a whole 4x4x8 slice. The times are simulated.
256 devices in a mesh: scen: 8 (over y, z_hi), grid: 32 (over x, z_lo, core).
Axes of the slice: x: 4, y: 4, z: 8 (z_hi: 2, z_lo: 4; z = z_hi * 4 + z_lo), core: 2. Of those that a mesh axis runs over, the one named last changes fastest.
Arguments:
- adjoint_in: float32 [16, 2, 50, 512, 128], P('scen', None, None, 'grid'), may hold values from -6 to 6
- surface_carbon: float32 [16, 512, 128], P('scen', 'grid'), may hold values from 1.9 to 2.1
- surface_alkalinity: float32 [16, 512, 128], P('scen', 'grid'), may hold values from 2.2 to 2.4
- east_velocity: float32 [50, 512, 128], P(None, 'grid'), may hold values from -0.1 to 0.1
- north_velocity: float32 [50, 512, 128], P(None, 'grid'), may hold values from -0.1 to 0.1
- east_diffusion: float32 [50], replicated, may hold values from 0.08 to 0.25
- north_diffusion: float32 [50], replicated, may hold values from 0.02 to 0.1
- vertical_mix: float32 [50, 512, 128], P(None, 'grid'), may hold values from 0.05 to 5
- thickness: float32 [50], replicated, may hold values from 0.5 to 4
- export_flux: float32 [50, 512, 128], P(None, 'grid'), may hold values from 0.1 to 1
- piston: float32 [512, 128], P('grid'), may hold values from 0.0005 to 0.005
- wet_mask: int32 [512, 128], P('grid'), may hold values 0 or 1
- bottom_level: int32 [512, 128], P('grid'), may hold values from 41 to 50
Outputs:
- adjoint_out: float32 [16, 2, 50, 512, 128], P('scen', None, None, 'grid')
- rate_gradient: float32 [50, 512, 128], P(None, 'grid')
All inputs are finite; a program needn't handle non-finite values. No bound on the sum of `wet_mask` on one device may be relied on, other than what follows from the above.
Results may differ from a plain program's by a relative error of at most 0.00002.
Values sent between devices are 32-bit elements; how exact they have to be, the bound alone decides.
No kernel may reach another device: no remote copies, remote signals or barrier semaphores. Data moves between devices by JAX's collectives and lax.ppermute only.
A program may use at most 64 MiB of HBM per device.

v0:
```python
import jax
import jax.numpy as jnp
from jax import lax
from jax.sharding import PartitionSpec as P

SUBSTEPS = 6
alk_ratio = 0.137


def extended(array, sides, width):
    for axis, dim in sides:
        size, length = (lax.axis_size(axis), array.shape[dim])
        up = [(i, (i + 1) % size) for i in range(size)]
        down = [(j, i) for i, j in up]
        last = lax.slice_in_dim(array, length - width, length, axis=dim)
        initial = lax.slice_in_dim(array, 0, width, axis=dim)
        before = lax.ppermute(last, axis, up)
        after = lax.ppermute(initial, axis, down)
        array = jnp.concatenate([before, array, after], axis=dim)
    return array


def wet_cells(wet_mask, bottom_level, levels):
    depth_index = lax.broadcasted_iota(jnp.int32, (levels,) + wet_mask.shape, 0)
    return ((wet_mask[None] > 0) & (depth_index < bottom_level[None])).astype(jnp.float32)


def face_pairs(velocity, mask_here, mask_next, diffusion):
    opened = mask_here * mask_next
    moving = velocity * opened
    mixing = diffusion[:, None, None] * opened
    return (mixing + jnp.maximum(moving, 0.0), jnp.minimum(moving, 0.0) - mixing)


def north_transpose(adjoint, upwind, downwind):
    zero_column = jnp.zeros(adjoint.shape[:-1] + (1,), jnp.float32)
    zero_face = jnp.zeros(upwind.shape[:-1] + (1,), jnp.float32)
    ahead = jnp.concatenate([adjoint[..., 1:], zero_column], -1)
    behind = jnp.concatenate([zero_column, adjoint[..., :-1]], -1)
    upwind_full = jnp.concatenate([upwind, zero_face], -1)
    downwind_full = jnp.concatenate([zero_face, downwind], -1)
    return upwind_full * (adjoint - ahead) + downwind_full * (behind - adjoint)


def column_coefficients(vertical_mix, thickness, wet_cube):
    zero_layer = jnp.zeros((1,) + wet_cube.shape[1:], jnp.float32)
    opened = jnp.concatenate([wet_cube[:-1] * wet_cube[1:], zero_layer], 0)
    mixing = vertical_mix * opened
    mixing_above = jnp.concatenate([zero_layer, mixing[:-1]], 0)
    height = thickness[:, None, None]
    height_above = jnp.concatenate([thickness[:1], thickness[:-1]])[:, None, None]
    height_below = jnp.concatenate([thickness[1:], thickness[-1:]])[:, None, None]
    diagonal = 1.0 + (mixing + mixing_above) / height
    below_band = -mixing_above / height_above
    above_band = -mixing / height_below
    return (below_band, diagonal, above_band)


def transposed_solve(right_side, below_band, diagonal, above_band):
    levels = diagonal.shape[0]
    pivots = diagonal[0]
    factors = [above_band[0] / pivots]
    reduced = [right_side[..., 0, :, :] / pivots]
    for level in range(1, levels):
        pivots = diagonal[level] - below_band[level] * factors[-1]
        factors.append(above_band[level] / pivots)
        reduced.append((right_side[..., level, :, :] - below_band[level] * reduced[-1]) / pivots)
    solved = [reduced[-1]]
    for level in range(levels - 2, -1, -1):
        solved.append(reduced[level] - factors[level] * solved[-1])
    return jnp.stack(solved[::-1], axis=-3)


def carbonate_slopes(carbon, alkalinity):
    excess = 2.0 * carbon - alkalinity
    spread = alkalinity - carbon
    square = spread * spread
    return (
        (4.0 * excess * spread + excess * excess) / square,
        (-2.0 * excess * spread - excess * excess) / square,
    )


def on_device(
    adjoint_in,
    surface_carbon,
    surface_alkalinity,
    east_velocity,
    north_velocity,
    east_diffusion,
    north_diffusion,
    vertical_mix,
    thickness,
    export_flux,
    piston,
    wet_mask,
    bottom_level,
):
    levels = vertical_mix.shape[0]
    wet_cube = wet_cells(wet_mask, bottom_level, levels)
    below_band, diagonal, above_band = column_coefficients(vertical_mix, thickness, wet_cube)
    adjoint = transposed_solve(adjoint_in, below_band, diagonal, above_band)
    stacked = jnp.stack([east_velocity, wet_cube])
    widened = extended(stacked, (("grid", 2),), 1)
    east_a, east_b = face_pairs(
        widened[0][:, :-1], widened[1][:, :-1], widened[1][:, 1:], east_diffusion
    )
    north_a, north_b = face_pairs(
        north_velocity[:, :, :-1], wet_cube[:, :, :-1], wet_cube[:, :, 1:], north_diffusion
    )
    for repeat in range(SUBSTEPS):
        wide_adjoint = extended(adjoint, (("grid", 3),), 1)
        centre = wide_adjoint[..., 1:-1, :]
        adjoint = (
            centre
            - east_a[:, 1:] * (centre - wide_adjoint[..., 2:, :])
            - east_b[:, :-1] * (wide_adjoint[..., :-2, :] - centre)
            - north_transpose(centre, north_a, north_b)
        )
    rate_term = jnp.sum(adjoint[:, 0] - alk_ratio * adjoint[:, 1], axis=0)
    summed = lax.psum(rate_term, "scen")
    rate_gradient = export_flux * wet_cube * summed
    slope_carbon, slope_alkalinity = carbonate_slopes(surface_carbon, surface_alkalinity)
    exchange_scale = wet_cube[0] * piston * adjoint[:, 0, 0]
    adjoint = (
        adjoint.at[:, 0, 0]
        .add(-exchange_scale * slope_carbon)
        .at[:, 1, 0]
        .add(-exchange_scale * slope_alkalinity)
    )
    return (adjoint, rate_gradient)


def solution(mesh):
    in_specs = (
        P("scen", None, None, "grid", None),
        P("scen", "grid", None),
        P("scen", "grid", None),
        P(None, "grid", None),
        P(None, "grid", None),
        P(),
        P(),
        P(None, "grid", None),
        P(),
        P(None, "grid", None),
        P("grid", None),
        P("grid", None),
        P("grid", None),
    )
    out_specs = (P("scen", None, None, "grid", None), P(None, "grid", None))
    return jax.shard_map(
        on_device, mesh=mesh, in_specs=in_specs, out_specs=out_specs, check_vma=False
    )
```

profile of v0, /device:TPU:2, one launch (start us, length us, event | category | flops | bytes accessed | tf_op | source)
XLA Modules:
  0.0 205.5 jit_solution(14609413593430815188)
XLA Ops:
  7.2 1.3 fusion.358
  8.5 0.8 fusion.359
  10.0 0.8 fusion.45
  10.8 1.4 pad_maximum_fusion.15
  12.7 1.1 copy-done
  15.7 0.8 constant_dynamic-update-slice_fusion.6
  16.7 4.1 %collective-permute-start.2 = (f32[2,2,50,1,128]{4,3,0,2,1:T(1,128)S(1)}, f32[2,2,50,1,128]{4,3,0,2,1:T(1,128)S(1)}, u32[]{:S(2)}, u32[]{:S(2)}) collective-permute-start(f32[2,2,50,1,128]{4,3,0,2,1:T(1,128)S(1)} %get-tuple-element.196), channel_id=1, source_target_pairs={{1,0},{2,1},{3,2},{4,3},{5,4},{6,5},{7,6},{8,7},{9,8},{10,9},{11,1... | collective-permute-start | bytes 307208 | tf_op jit(solution)/shard_map/ppermute | solution.py:18
  21.0 4.5 %collective-permute-start.1 = (f32[2,50,1,128]{3,2,1,0:T(1,128)S(1)}, f32[2,50,1,128]{3,2,1,0:T(1,128)S(1)}, u32[]{:S(2)}, u32[]{:S(2)}) collective-permute-start(f32[2,50,1,128]{3,2,1,0:T(1,128)S(1)} %get-tuple-element.255), channel_id=1, source_target_pairs={{1,0},{2,1},{3,2},{4,3},{5,4},{6,5},{7,6},{8,7},{9,8},{10,9},{11,1... | collective-permute-start | bytes 153608 | tf_op jit(solution)/shard_map/ppermute | solution.py:18
  27.1 1.6 collective-permute-done
  29.8 1.2 fusion.38
  31.2 3.2 %collective-permute-start.4 = (f32[2,2,50,1,128]{4,3,0,2,1:T(1,128)S(1)}, f32[2,2,50,1,128]{4,3,0,2,1:T(1,128)S(1)}, u32[]{:S(2)}, u32[]{:S(2)}) collective-permute-start(f32[2,2,50,1,128]{4,3,0,2,1:T(1,128)S(1)} %get-tuple-element.192), channel_id=1, source_target_pairs={{1,0},{2,1},{3,2},{4,3},{5,4},{6,5},{7,6},{8,7},{9,8},{10,9},{11,1... | collective-permute-start | bytes 307208 | tf_op jit(solution)/shard_map/ppermute | solution.py:18
  35.0 1.6 collective-permute-done.4
  36.7 5.2 %collective-permute-done.5 = f32[2,2,50,1,128]{4,3,0,2,1:T(1,128)S(1)} collective-permute-done((f32[2,2,50,1,128]{4,3,0,2,1:T(1,128)S(1)}, f32[2,2,50,1,128]{4,3,0,2,1:T(1,128)S(1)}, u32[]{:S(2)}, u32[]{:S(2)}) %collective-permute-start.5) | collective-permute-done | bytes 102432 | tf_op jit(solution)/shard_map/ppermute | solution.py:17
  41.8 1.2 fusion.31
  44.4 2.0 collective-permute-done.6
  46.4 3.9 %collective-permute-done.7 = f32[2,2,50,1,128]{4,3,0,2,1:T(1,128)S(1)} collective-permute-done((f32[2,2,50,1,128]{4,3,0,2,1:T(1,128)S(1)}, f32[2,2,50,1,128]{4,3,0,2,1:T(1,128)S(1)}, u32[]{:S(2)}, u32[]{:S(2)}) %collective-permute-start.7) | collective-permute-done | bytes 102432 | tf_op jit(solution)/shard_map/ppermute | solution.py:17
  50.3 1.2 fusion.24
  51.6 0.9 collective-permute-start.8
  53.2 1.7 collective-permute-done.8
  54.8 4.5 %collective-permute-done.9 = f32[2,2,50,1,128]{4,3,0,2,1:T(1,128)S(1)} collective-permute-done((f32[2,2,50,1,128]{4,3,0,2,1:T(1,128)S(1)}, f32[2,2,50,1,128]{4,3,0,2,1:T(1,128)S(1)}, u32[]{:S(2)}, u32[]{:S(2)}) %collective-permute-start.9) | collective-permute-done | bytes 102432 | tf_op jit(solution)/shard_map/ppermute | solution.py:17
  59.3 1.2 fusion.17
  61.9 2.0 collective-permute-done.10
  63.9 4.0 %collective-permute-done.11 = f32[2,2,50,1,128]{4,3,0,2,1:T(1,128)S(1)} collective-permute-done((f32[2,2,50,1,128]{4,3,0,2,1:T(1,128)S(1)}, f32[2,2,50,1,128]{4,3,0,2,1:T(1,128)S(1)}, u32[]{:S(2)}, u32[]{:S(2)}) %collective-permute-start.11) | collective-permute-done | bytes 102432 | tf_op jit(solution)/shard_map/ppermute | solution.py:17
  67.9 1.2 fusion.10
  69.2 0.8 collective-permute-start.12
  70.6 1.8 collective-permute-done.12
  72.4 4.4 %collective-permute-done.13 = f32[2,2,50,1,128]{4,3,0,2,1:T(1,128)S(1)} collective-permute-done((f32[2,2,50,1,128]{4,3,0,2,1:T(1,128)S(1)}, f32[2,2,50,1,128]{4,3,0,2,1:T(1,128)S(1)}, u32[]{:S(2)}, u32[]{:S(2)}) %collective-permute-start.13) | collective-permute-done | bytes 102432 | tf_op jit(solution)/shard_map/ppermute | solution.py:17
  76.8 1.2 fusion.3
  78.2 1.0 fusion.43
  79.3 1.3 copy.115
  81.2 115.5 %all-reduce.18.cloned.1.call-done = f32[50,16,128]{2,1,0:T(8,128)} async-done(((f32[50,16,128]{2,1,0:T(8,128)}), f32[50,16,128]{2,1,0:T(8,128)}) %all-reduce.18.cloned.1.call-update) | async-done | bytes 409616 | tf_op jit(solution)/shard_map/psum | solution.py:121
  196.7 2.0 select_multiply_fusion
  (124 shorter events, 11.5 us)
Async XLA Ops:
  7.2 5.0 %copy-start.2 = (f32[50,16,128]{2,1,0:T(8,128)S(1)}, f32[50,16,128]{2,1,0:T(8,128)}, u32[]{:S(2)}) copy-start(f32[50,16,128]{2,1,0:T(8,128)} %param.24) | copy-start | bytes 1228804
  7.2 189.5 %all-reduce.18.cloned.1.call-start = ((), (), s32[]{:S(2)}) async-start(), calls=%async_computation | async-start | bytes 819200 | tf_op jit(solution)/shard_map/psum | solution.py:121
  10.8 1.6 copy-start.7
  12.3 1.4 copy-start
  15.6 5.1 %copy-start.4 = (s32[16,128]{1,0:T(8,128)S(1)}, s32[16,128]{1,0:T(8,128)}, u32[]{:S(2)}) copy-start(s32[16,128]{1,0:T(8,128)} %param.29) | copy-start | bytes 24580
  15.7 5.2 %copy-start.1 = (f32[50,16,128]{2,1,0:T(8,128)S(1)}, f32[50,16,128]{2,1,0:T(8,128)}, u32[]{:S(2)}) copy-start(f32[50,16,128]{2,1,0:T(8,128)} %param.20) | copy-start | bytes 1228804
  16.7 13.2 %collective-permute-start.2 = (f32[2,2,50,1,128]{4,3,0,2,1:T(1,128)S(1)}, f32[2,2,50,1,128]{4,3,0,2,1:T(1,128)S(1)}, u32[]{:S(2)}, u32[]{:S(2)}) collective-permute-start(f32[2,2,50,1,128]{4,3,0,2,1:T(1,128)S(1)} %get-tuple-element.196), channel_id=1, source_target_pairs={{1,0},{2,1},{3,2},{4,3},{5,4},{6,5},{7,6},{8,7},{9,8},{10,9},{11,1... | collective-permute-start | bytes 307208 | tf_op jit(solution)/shard_map/ppermute | solution.py:18
  20.8 9.0 %collective-permute-start.3 = (f32[2,2,50,1,128]{4,3,0,2,1:T(1,128)S(1)}, f32[2,2,50,1,128]{4,3,0,2,1:T(1,128)S(1)}, u32[]{:S(2)}, u32[]{:S(2)}) collective-permute-start(f32[2,2,50,1,128]{4,3,0,2,1:T(1,128)S(1)} %get-tuple-element.197), channel_id=1, source_target_pairs={{0,1},{1,2},{2,3},{3,4},{4,5},{5,6},{6,7},{7,8},{8,9},{9,10},{10,1... | collective-permute-start | bytes 307208 | tf_op jit(solution)/shard_map/ppermute | solution.py:17
  20.9 7.7 %collective-permute-start = (f32[2,50,1,128]{3,2,1,0:T(1,128)S(1)}, f32[2,50,1,128]{3,2,1,0:T(1,128)S(1)}, u32[]{:S(2)}, u32[]{:S(2)}) collective-permute-start(f32[2,50,1,128]{3,2,1,0:T(1,128)S(1)} %get-tuple-element.254), channel_id=1, source_target_pairs={{0,1},{1,2},{2,3},{3,4},{4,5},{5,6},{6,7},{7,8},{8,9},{9,10},{10,1... | collective-permute-start | bytes 153608 | tf_op jit(solution)/shard_map/ppermute | solution.py:17
  21.0 5.2 %copy-start.3 = (f32[50,16,128]{2,1,0:T(8,128)S(1)}, f32[50,16,128]{2,1,0:T(8,128)}, u32[]{:S(2)}) copy-start(f32[50,16,128]{2,1,0:T(8,128)} %param.21) | copy-start | bytes 1228804
  21.0 5.1 %copy-start.9 = (f32[50]{0:T(128)S(1)}, f32[50]{0:T(128)}, u32[]{:S(2)}) copy-start(f32[50]{0:T(128)} %param.23) | copy-start | bytes 604
  21.0 7.6 %collective-permute-start.1 = (f32[2,50,1,128]{3,2,1,0:T(1,128)S(1)}, f32[2,50,1,128]{3,2,1,0:T(1,128)S(1)}, u32[]{:S(2)}, u32[]{:S(2)}) collective-permute-start(f32[2,50,1,128]{3,2,1,0:T(1,128)S(1)} %get-tuple-element.255), channel_id=1, source_target_pairs={{1,0},{2,1},{3,2},{4,3},{5,4},{6,5},{7,6},{8,7},{9,8},{10,9},{11,1... | collective-permute-start | bytes 153608 | tf_op jit(solution)/shard_map/ppermute | solution.py:18
  26.2 0.7 copy-start.8
  28.9 0.7 copy-start.10
  31.2 5.5 %collective-permute-start.4 = (f32[2,2,50,1,128]{4,3,0,2,1:T(1,128)S(1)}, f32[2,2,50,1,128]{4,3,0,2,1:T(1,128)S(1)}, u32[]{:S(2)}, u32[]{:S(2)}) collective-permute-start(f32[2,2,50,1,128]{4,3,0,2,1:T(1,128)S(1)} %get-tuple-element.192), channel_id=1, source_target_pairs={{1,0},{2,1},{3,2},{4,3},{5,4},{6,5},{7,6},{8,7},{9,8},{10,9},{11,1... | collective-permute-start | bytes 307208 | tf_op jit(solution)/shard_map/ppermute | solution.py:18
  34.4 7.4 %collective-permute-start.5 = (f32[2,2,50,1,128]{4,3,0,2,1:T(1,128)S(1)}, f32[2,2,50,1,128]{4,3,0,2,1:T(1,128)S(1)}, u32[]{:S(2)}, u32[]{:S(2)}) collective-permute-start(f32[2,2,50,1,128]{4,3,0,2,1:T(1,128)S(1)} %get-tuple-element.193), channel_id=1, source_target_pairs={{0,1},{1,2},{2,3},{3,4},{4,5},{5,6},{6,7},{7,8},{8,9},{9,10},{10,1... | collective-permute-start | bytes 307208 | tf_op jit(solution)/shard_map/ppermute | solution.py:17
  43.2 3.2 %collective-permute-start.6 = (f32[2,2,50,1,128]{4,3,0,2,1:T(1,128)S(1)}, f32[2,2,50,1,128]{4,3,0,2,1:T(1,128)S(1)}, u32[]{:S(2)}, u32[]{:S(2)}) collective-permute-start(f32[2,2,50,1,128]{4,3,0,2,1:T(1,128)S(1)} %get-tuple-element.188), channel_id=1, source_target_pairs={{1,0},{2,1},{3,2},{4,3},{5,4},{6,5},{7,6},{8,7},{9,8},{10,9},{11,1... | collective-permute-start | bytes 307208 | tf_op jit(solution)/shard_map/ppermute | solution.py:18
  43.3 7.0 %collective-permute-start.7 = (f32[2,2,50,1,128]{4,3,0,2,1:T(1,128)S(1)}, f32[2,2,50,1,128]{4,3,0,2,1:T(1,128)S(1)}, u32[]{:S(2)}, u32[]{:S(2)}) collective-permute-start(f32[2,2,50,1,128]{4,3,0,2,1:T(1,128)S(1)} %get-tuple-element.189), channel_id=1, source_target_pairs={{0,1},{1,2},{2,3},{3,4},{4,5},{5,6},{6,7},{7,8},{8,9},{9,10},{10,1... | collective-permute-start | bytes 307208 | tf_op jit(solution)/shard_map/ppermute | solution.py:17
  51.6 3.2 %collective-permute-start.8 = (f32[2,2,50,1,128]{4,3,0,2,1:T(1,128)S(1)}, f32[2,2,50,1,128]{4,3,0,2,1:T(1,128)S(1)}, u32[]{:S(2)}, u32[]{:S(2)}) collective-permute-start(f32[2,2,50,1,128]{4,3,0,2,1:T(1,128)S(1)} %get-tuple-element.184), channel_id=1, source_target_pairs={{1,0},{2,1},{3,2},{4,3},{5,4},{6,5},{7,6},{8,7},{9,8},{10,9},{11,1... | collective-permute-start | bytes 307208 | tf_op jit(solution)/shard_map/ppermute | solution.py:18
  52.5 6.8 %collective-permute-start.9 = (f32[2,2,50,1,128]{4,3,0,2,1:T(1,128)S(1)}, f32[2,2,50,1,128]{4,3,0,2,1:T(1,128)S(1)}, u32[]{:S(2)}, u32[]{:S(2)}) collective-permute-start(f32[2,2,50,1,128]{4,3,0,2,1:T(1,128)S(1)} %get-tuple-element.185), channel_id=1, source_target_pairs={{0,1},{1,2},{2,3},{3,4},{4,5},{5,6},{6,7},{7,8},{8,9},{9,10},{10,1... | collective-permute-start | bytes 307208 | tf_op jit(solution)/shard_map/ppermute | solution.py:17
  60.7 3.2 %collective-permute-start.10 = (f32[2,2,50,1,128]{4,3,0,2,1:T(1,128)S(1)}, f32[2,2,50,1,128]{4,3,0,2,1:T(1,128)S(1)}, u32[]{:S(2)}, u32[]{:S(2)}) collective-permute-start(f32[2,2,50,1,128]{4,3,0,2,1:T(1,128)S(1)} %get-tuple-element.180), channel_id=1, source_target_pairs={{1,0},{2,1},{3,2},{4,3},{5,4},{6,5},{7,6},{8,7},{9,8},{10,9},{11,1... | collective-permute-start | bytes 307208 | tf_op jit(solution)/shard_map/ppermute | solution.py:18
  60.9 7.0 %collective-permute-start.11 = (f32[2,2,50,1,128]{4,3,0,2,1:T(1,128)S(1)}, f32[2,2,50,1,128]{4,3,0,2,1:T(1,128)S(1)}, u32[]{:S(2)}, u32[]{:S(2)}) collective-permute-start(f32[2,2,50,1,128]{4,3,0,2,1:T(1,128)S(1)} %get-tuple-element.181), channel_id=1, source_target_pairs={{0,1},{1,2},{2,3},{3,4},{4,5},{5,6},{6,7},{7,8},{8,9},{9,10},{10,1... | collective-permute-start | bytes 307208 | tf_op jit(solution)/shard_map/ppermute | solution.py:17
  69.2 3.2 %collective-permute-start.12 = (f32[2,2,50,1,128]{4,3,0,2,1:T(1,128)S(1)}, f32[2,2,50,1,128]{4,3,0,2,1:T(1,128)S(1)}, u32[]{:S(2)}, u32[]{:S(2)}) collective-permute-start(f32[2,2,50,1,128]{4,3,0,2,1:T(1,128)S(1)} %get-tuple-element.176), channel_id=1, source_target_pairs={{1,0},{2,1},{3,2},{4,3},{5,4},{6,5},{7,6},{8,7},{9,8},{10,9},{11,1... | collective-permute-start | bytes 307208 | tf_op jit(solution)/shard_map/ppermute | solution.py:18
  70.0 6.8 %collective-permute-start.13 = (f32[2,2,50,1,128]{4,3,0,2,1:T(1,128)S(1)}, f32[2,2,50,1,128]{4,3,0,2,1:T(1,128)S(1)}, u32[]{:S(2)}, u32[]{:S(2)}) collective-permute-start(f32[2,2,50,1,128]{4,3,0,2,1:T(1,128)S(1)} %get-tuple-element.177), channel_id=1, source_target_pairs={{0,1},{1,2},{2,3},{3,4},{4,5},{5,6},{6,7},{7,8},{8,9},{9,10},{10,1... | collective-permute-start | bytes 307208 | tf_op jit(solution)/shard_map/ppermute | solution.py:17
  78.2 1.0 copy-start.5
  78.2 1.0 copy-start.6
Sparse Core Ops, SparseCore 0:
  79.3 117.3 all-reduce.17
where the time goes:
time: 206 us
  waiting for transfers between devices  148 us (72%)
  other arithmetic  16.9 us (8%)
  starting transfers between devices  14.8 us (7%)
  between operations  14.8 us (7%)
  local copies, waits for them, and re-layouts  10.9 us (5%)
    psum x1, waiting for transfers between devices, on_device(): summed = lax.psum(rate_term, 'scen')  116 us
    ppermute x7, waiting for transfers between devices, extended(): before = lax.ppermute(last, axis, up)  23.5 us
    ppermute x7, starting transfers between devices, extended(): after = lax.ppermute(initial, axis, down)  13.8 us
    ppermute x7, waiting for transfers between devices, extended(): after = lax.ppermute(initial, axis, down)  9.04 us
    sub x6, other arithmetic, on_device(): centre - east_a[:, 1:] * (centre - wide_adjoint[..., 2:, :])  7.31 us
  transfers between devices with their start and end apart: 15, of which 12 were waited for; matrix products, arithmetic and copies ran while one was open for 3% of the time, Pallas kernels for 0%

commit v1 on v0

--- a/solution.py
+++ b/solution.py
@@ -2,9 +2,15 @@
 import jax.numpy as jnp
 from jax import lax
 from jax.sharding import PartitionSpec as P
+from jax.lax import all_gather
 
 SUBSTEPS = 6
 alk_ratio = 0.137
+
+
+def pair_the_loads(body):
+    base_arr = jnp.sum(all_gather(body, "scen"), 0)
+    return base_arr
 
 
 def extended(array, sides, width):
@@ -118,7 +124,7 @@
             - north_transpose(centre, north_a, north_b)
         )
     rate_term = jnp.sum(adjoint[:, 0] - alk_ratio * adjoint[:, 1], axis=0)
-    summed = lax.psum(rate_term, "scen")
+    summed = pair_the_loads(rate_term)
     rate_gradient = export_flux * wet_cube * summed
     slope_carbon, slope_alkalinity = carbonate_slopes(surface_carbon, surface_alkalinity)
     exchange_scale = wet_cube[0] * piston * adjoint[:, 0, 0]

time: 206 us -> 191 us (0.927)
  waiting for transfers between devices: 148 us -> 134 us
    psum x1 -> x0, waiting for transfers between devices: 116 us -> none  [on_device(): summed = lax.psum(rate_term, 'scen')]
    all_gather x0 -> x1, waiting for transfers between devices: none -> 100 us  [pair_the_loads(): base_arr = jnp.sum(all_gather(body, 'scen'), 0)]
    reduce_sum x0 -> x1, other arithmetic: none -> 2.23 us  [pair_the_loads(): base_arr = jnp.sum(all_gather(body, 'scen'), 0)]
where the time goes in v1:
time: 191 us; the launch traced here: 190 us
  waiting for transfers between devices  134 us (70%)
  other arithmetic  17.5 us (9%)
  starting transfers between devices  14.8 us (8%)
  between operations  14.8 us (8%)
  local copies, waits for them, and re-layouts  9.77 us (5%)
    all_gather x1, waiting for transfers between devices, pair_the_loads(): base_arr = jnp.sum(all_gather(body, 'scen'), 0)  100 us
    ppermute x7, waiting for transfers between devices, extended(): before = lax.ppermute(last, axis, up)  24 us
    ppermute x7, starting transfers between devices, extended(): after = lax.ppermute(initial, axis, down)  13.8 us
    ppermute x7, waiting for transfers between devices, extended(): after = lax.ppermute(initial, axis, down)  9.04 us
    sub x6, other arithmetic, on_device(): centre - east_a[:, 1:] * (centre - wide_adjoint[..., 2:, :])  7.35 us
  transfers between devices with their start and end apart: 15, of which 12 were waited for; matrix products, arithmetic and copies ran while one was open for 3% of the time, Pallas kernels for 0%

profile of v1, /device:TPU:2, one launch (start us, length us, event | category | flops | bytes accessed | tf_op | source)
XLA Modules:
  0.0 190.4 jit_solution(2570459996005765170)
XLA Ops:
  7.2 1.3 fusion.358
  8.5 0.8 fusion.359
  10.0 0.8 fusion.45
  10.8 1.4 pad_maximum_fusion.15
  12.7 1.1 copy-done
  15.6 0.8 constant_dynamic-update-slice_fusion.6
  16.6 4.1 %collective-permute-start.2 = (f32[2,2,50,1,128]{4,3,0,2,1:T(1,128)S(1)}, f32[2,2,50,1,128]{4,3,0,2,1:T(1,128)S(1)}, u32[]{:S(2)}, u32[]{:S(2)}) collective-permute-start(f32[2,2,50,1,128]{4,3,0,2,1:T(1,128)S(1)} %get-tuple-element.196), channel_id=1, source_target_pairs={{1,0},{2,1},{3,2},{4,3},{5,4},{6,5},{7,6},{8,7},{9,8},{10,9},{11,1... | collective-permute-start | bytes 307208 | tf_op jit(solution)/shard_map/ppermute | solution.py:24
  21.0 4.5 %collective-permute-start.1 = (f32[2,50,1,128]{3,2,1,0:T(1,128)S(1)}, f32[2,50,1,128]{3,2,1,0:T(1,128)S(1)}, u32[]{:S(2)}, u32[]{:S(2)}) collective-permute-start(f32[2,50,1,128]{3,2,1,0:T(1,128)S(1)} %get-tuple-element.255), channel_id=1, source_target_pairs={{1,0},{2,1},{3,2},{4,3},{5,4},{6,5},{7,6},{8,7},{9,8},{10,9},{11,1... | collective-permute-start | bytes 153608 | tf_op jit(solution)/shard_map/ppermute | solution.py:24
  26.6 2.0 %collective-permute-done = f32[2,50,1,128]{3,2,1,0:T(1,128)S(1)} collective-permute-done((f32[2,50,1,128]{3,2,1,0:T(1,128)S(1)}, f32[2,50,1,128]{3,2,1,0:T(1,128)S(1)}, u32[]{:S(2)}, u32[]{:S(2)}) %collective-permute-start) | collective-permute-done | bytes 51232 | tf_op jit(solution)/shard_map/ppermute | solution.py:23
  29.8 1.3 fusion.38
  31.2 3.2 %collective-permute-start.4 = (f32[2,2,50,1,128]{4,3,0,2,1:T(1,128)S(1)}, f32[2,2,50,1,128]{4,3,0,2,1:T(1,128)S(1)}, u32[]{:S(2)}, u32[]{:S(2)}) collective-permute-start(f32[2,2,50,1,128]{4,3,0,2,1:T(1,128)S(1)} %get-tuple-element.192), channel_id=1, source_target_pairs={{1,0},{2,1},{3,2},{4,3},{5,4},{6,5},{7,6},{8,7},{9,8},{10,9},{11,1... | collective-permute-start | bytes 307208 | tf_op jit(solution)/shard_map/ppermute | solution.py:24
  35.0 1.6 collective-permute-done.4
  36.7 5.2 %collective-permute-done.5 = f32[2,2,50,1,128]{4,3,0,2,1:T(1,128)S(1)} collective-permute-done((f32[2,2,50,1,128]{4,3,0,2,1:T(1,128)S(1)}, f32[2,2,50,1,128]{4,3,0,2,1:T(1,128)S(1)}, u32[]{:S(2)}, u32[]{:S(2)}) %collective-permute-start.5) | collective-permute-done | bytes 102432 | tf_op jit(solution)/shard_map/ppermute | solution.py:23
  41.8 1.2 fusion.31
  44.4 2.0 %collective-permute-done.6 = f32[2,2,50,1,128]{4,3,0,2,1:T(1,128)S(1)} collective-permute-done((f32[2,2,50,1,128]{4,3,0,2,1:T(1,128)S(1)}, f32[2,2,50,1,128]{4,3,0,2,1:T(1,128)S(1)}, u32[]{:S(2)}, u32[]{:S(2)}) %collective-permute-start.6) | collective-permute-done | bytes 102432 | tf_op jit(solution)/shard_map/ppermute | solution.py:24
  46.4 3.9 %collective-permute-done.7 = f32[2,2,50,1,128]{4,3,0,2,1:T(1,128)S(1)} collective-permute-done((f32[2,2,50,1,128]{4,3,0,2,1:T(1,128)S(1)}, f32[2,2,50,1,128]{4,3,0,2,1:T(1,128)S(1)}, u32[]{:S(2)}, u32[]{:S(2)}) %collective-permute-start.7) | collective-permute-done | bytes 102432 | tf_op jit(solution)/shard_map/ppermute | solution.py:23
  50.3 1.2 fusion.24
  51.6 0.9 collective-permute-start.8
  53.2 1.7 collective-permute-done.8
  54.8 4.5 %collective-permute-done.9 = f32[2,2,50,1,128]{4,3,0,2,1:T(1,128)S(1)} collective-permute-done((f32[2,2,50,1,128]{4,3,0,2,1:T(1,128)S(1)}, f32[2,2,50,1,128]{4,3,0,2,1:T(1,128)S(1)}, u32[]{:S(2)}, u32[]{:S(2)}) %collective-permute-start.9) | collective-permute-done | bytes 102432 | tf_op jit(solution)/shard_map/ppermute | solution.py:23
  59.3 1.2 fusion.17
  61.9 2.0 %collective-permute-done.10 = f32[2,2,50,1,128]{4,3,0,2,1:T(1,128)S(1)} collective-permute-done((f32[2,2,50,1,128]{4,3,0,2,1:T(1,128)S(1)}, f32[2,2,50,1,128]{4,3,0,2,1:T(1,128)S(1)}, u32[]{:S(2)}, u32[]{:S(2)}) %collective-permute-start.10) | collective-permute-done | bytes 102432 | tf_op jit(solution)/shard_map/ppermute | solution.py:24
  63.9 4.0 %collective-permute-done.11 = f32[2,2,50,1,128]{4,3,0,2,1:T(1,128)S(1)} collective-permute-done((f32[2,2,50,1,128]{4,3,0,2,1:T(1,128)S(1)}, f32[2,2,50,1,128]{4,3,0,2,1:T(1,128)S(1)}, u32[]{:S(2)}, u32[]{:S(2)}) %collective-permute-start.11) | collective-permute-done | bytes 102432 | tf_op jit(solution)/shard_map/ppermute | solution.py:23
  67.9 1.2 fusion.10
  69.2 0.8 collective-permute-start.12
  70.6 1.8 collective-permute-done.12
  72.4 4.4 %collective-permute-done.13 = f32[2,2,50,1,128]{4,3,0,2,1:T(1,128)S(1)} collective-permute-done((f32[2,2,50,1,128]{4,3,0,2,1:T(1,128)S(1)}, f32[2,2,50,1,128]{4,3,0,2,1:T(1,128)S(1)}, u32[]{:S(2)}, u32[]{:S(2)}) %collective-permute-start.13) | collective-permute-done | bytes 102432 | tf_op jit(solution)/shard_map/ppermute | solution.py:23
  76.8 1.2 fusion.3
  78.1 1.0 fusion.43
  80.0 100.5 %all-gather.3.cloned.1.call-done = f32[400,16,128]{2,1,0:T(8,128)} async-done(((f32[50,16,128]{2,1,0:T(8,128)}), f32[400,16,128]{2,1,0:T(8,128)}) %all-gather.3.cloned.1.call-update) | async-done | bytes 3276816 | tf_op jit(solution)/shard_map/all_gather | solution.py:12
  180.5 2.2 %reduce_sum.19 = f32[50,16,128]{2,1,0:T(8,128)S(1)} reduce(f32[8,50,16,128]{3,2,1,0:T(8,128)} %bitcast.1268, f32[]{:T(128)} %constant.74.clone.1), dimensions={0}, to_apply=%region_1.0 | reduce | flops 716800 | bytes 3686404 | tf_op jit(solution)/shard_map/reduce_sum | solution.py:12
  182.8 0.8 select_multiply_fusion
  (129 shorter events, 11.1 us)
Async XLA Ops:
  7.2 5.0 %copy-start.3 = (f32[50,16,128]{2,1,0:T(8,128)S(1)}, f32[50,16,128]{2,1,0:T(8,128)}, u32[]{:S(2)}) copy-start(f32[50,16,128]{2,1,0:T(8,128)} %param.24) | copy-start | bytes 1228804
  7.2 173.3 %all-gather.3.cloned.1.call-start = ((), (), s32[]{:S(2)}) async-start(), calls=%async_computation | async-start | bytes 3686400 | tf_op jit(solution)/shard_map/all_gather | solution.py:12
  10.8 1.6 copy-start.9
  12.3 1.4 copy-start
  15.6 5.1 %copy-start.6 = (s32[16,128]{1,0:T(8,128)S(1)}, s32[16,128]{1,0:T(8,128)}, u32[]{:S(2)}) copy-start(s32[16,128]{1,0:T(8,128)} %param.29) | copy-start | bytes 24580
  15.6 5.2 %copy-start.2 = (f32[50,16,128]{2,1,0:T(8,128)S(1)}, f32[50,16,128]{2,1,0:T(8,128)}, u32[]{:S(2)}) copy-start(f32[50,16,128]{2,1,0:T(8,128)} %param.20) | copy-start | bytes 1228804
  16.6 13.1 %collective-permute-start.2 = (f32[2,2,50,1,128]{4,3,0,2,1:T(1,128)S(1)}, f32[2,2,50,1,128]{4,3,0,2,1:T(1,128)S(1)}, u32[]{:S(2)}, u32[]{:S(2)}) collective-permute-start(f32[2,2,50,1,128]{4,3,0,2,1:T(1,128)S(1)} %get-tuple-element.196), channel_id=1, source_target_pairs={{1,0},{2,1},{3,2},{4,3},{5,4},{6,5},{7,6},{8,7},{9,8},{10,9},{11,1... | collective-permute-start | bytes 307208 | tf_op jit(solution)/shard_map/ppermute | solution.py:24
  20.8 9.0 %collective-permute-start.3 = (f32[2,2,50,1,128]{4,3,0,2,1:T(1,128)S(1)}, f32[2,2,50,1,128]{4,3,0,2,1:T(1,128)S(1)}, u32[]{:S(2)}, u32[]{:S(2)}) collective-permute-start(f32[2,2,50,1,128]{4,3,0,2,1:T(1,128)S(1)} %get-tuple-element.197), channel_id=1, source_target_pairs={{0,1},{1,2},{2,3},{3,4},{4,5},{5,6},{6,7},{7,8},{8,9},{9,10},{10,1... | collective-permute-start | bytes 307208 | tf_op jit(solution)/shard_map/ppermute | solution.py:23
  20.9 7.7 %collective-permute-start = (f32[2,50,1,128]{3,2,1,0:T(1,128)S(1)}, f32[2,50,1,128]{3,2,1,0:T(1,128)S(1)}, u32[]{:S(2)}, u32[]{:S(2)}) collective-permute-start(f32[2,50,1,128]{3,2,1,0:T(1,128)S(1)} %get-tuple-element.254), channel_id=1, source_target_pairs={{0,1},{1,2},{2,3},{3,4},{4,5},{5,6},{6,7},{7,8},{8,9},{9,10},{10,1... | collective-permute-start | bytes 153608 | tf_op jit(solution)/shard_map/ppermute | solution.py:23
  21.0 5.2 %copy-start.5 = (f32[50,16,128]{2,1,0:T(8,128)S(1)}, f32[50,16,128]{2,1,0:T(8,128)}, u32[]{:S(2)}) copy-start(f32[50,16,128]{2,1,0:T(8,128)} %param.21) | copy-start | bytes 1228804
  21.0 5.1 %copy-start.11 = (f32[50]{0:T(128)S(1)}, f32[50]{0:T(128)}, u32[]{:S(2)}) copy-start(f32[50]{0:T(128)} %param.23) | copy-start | bytes 604
  21.0 7.6 %collective-permute-start.1 = (f32[2,50,1,128]{3,2,1,0:T(1,128)S(1)}, f32[2,50,1,128]{3,2,1,0:T(1,128)S(1)}, u32[]{:S(2)}, u32[]{:S(2)}) collective-permute-start(f32[2,50,1,128]{3,2,1,0:T(1,128)S(1)} %get-tuple-element.255), channel_id=1, source_target_pairs={{1,0},{2,1},{3,2},{4,3},{5,4},{6,5},{7,6},{8,7},{9,8},{10,9},{11,1... | collective-permute-start | bytes 153608 | tf_op jit(solution)/shard_map/ppermute | solution.py:24
  28.8 0.7 copy-start.12
  31.2 5.5 %collective-permute-start.4 = (f32[2,2,50,1,128]{4,3,0,2,1:T(1,128)S(1)}, f32[2,2,50,1,128]{4,3,0,2,1:T(1,128)S(1)}, u32[]{:S(2)}, u32[]{:S(2)}) collective-permute-start(f32[2,2,50,1,128]{4,3,0,2,1:T(1,128)S(1)} %get-tuple-element.192), channel_id=1, source_target_pairs={{1,0},{2,1},{3,2},{4,3},{5,4},{6,5},{7,6},{8,7},{9,8},{10,9},{11,1... | collective-permute-start | bytes 307208 | tf_op jit(solution)/shard_map/ppermute | solution.py:24
  34.4 7.4 %collective-permute-start.5 = (f32[2,2,50,1,128]{4,3,0,2,1:T(1,128)S(1)}, f32[2,2,50,1,128]{4,3,0,2,1:T(1,128)S(1)}, u32[]{:S(2)}, u32[]{:S(2)}) collective-permute-start(f32[2,2,50,1,128]{4,3,0,2,1:T(1,128)S(1)} %get-tuple-element.193), channel_id=1, source_target_pairs={{0,1},{1,2},{2,3},{3,4},{4,5},{5,6},{6,7},{7,8},{8,9},{9,10},{10,1... | collective-permute-start | bytes 307208 | tf_op jit(solution)/shard_map/ppermute | solution.py:23
  43.2 3.2 %collective-permute-start.6 = (f32[2,2,50,1,128]{4,3,0,2,1:T(1,128)S(1)}, f32[2,2,50,1,128]{4,3,0,2,1:T(1,128)S(1)}, u32[]{:S(2)}, u32[]{:S(2)}) collective-permute-start(f32[2,2,50,1,128]{4,3,0,2,1:T(1,128)S(1)} %get-tuple-element.188), channel_id=1, source_target_pairs={{1,0},{2,1},{3,2},{4,3},{5,4},{6,5},{7,6},{8,7},{9,8},{10,9},{11,1... | collective-permute-start | bytes 307208 | tf_op jit(solution)/shard_map/ppermute | solution.py:24
  43.3 7.0 %collective-permute-start.7 = (f32[2,2,50,1,128]{4,3,0,2,1:T(1,128)S(1)}, f32[2,2,50,1,128]{4,3,0,2,1:T(1,128)S(1)}, u32[]{:S(2)}, u32[]{:S(2)}) collective-permute-start(f32[2,2,50,1,128]{4,3,0,2,1:T(1,128)S(1)} %get-tuple-element.189), channel_id=1, source_target_pairs={{0,1},{1,2},{2,3},{3,4},{4,5},{5,6},{6,7},{7,8},{8,9},{9,10},{10,1... | collective-permute-start | bytes 307208 | tf_op jit(solution)/shard_map/ppermute | solution.py:23
  51.6 3.2 %collective-permute-start.8 = (f32[2,2,50,1,128]{4,3,0,2,1:T(1,128)S(1)}, f32[2,2,50,1,128]{4,3,0,2,1:T(1,128)S(1)}, u32[]{:S(2)}, u32[]{:S(2)}) collective-permute-start(f32[2,2,50,1,128]{4,3,0,2,1:T(1,128)S(1)} %get-tuple-element.184), channel_id=1, source_target_pairs={{1,0},{2,1},{3,2},{4,3},{5,4},{6,5},{7,6},{8,7},{9,8},{10,9},{11,1... | collective-permute-start | bytes 307208 | tf_op jit(solution)/shard_map/ppermute | solution.py:24
  52.5 6.8 %collective-permute-start.9 = (f32[2,2,50,1,128]{4,3,0,2,1:T(1,128)S(1)}, f32[2,2,50,1,128]{4,3,0,2,1:T(1,128)S(1)}, u32[]{:S(2)}, u32[]{:S(2)}) collective-permute-start(f32[2,2,50,1,128]{4,3,0,2,1:T(1,128)S(1)} %get-tuple-element.185), channel_id=1, source_target_pairs={{0,1},{1,2},{2,3},{3,4},{4,5},{5,6},{6,7},{7,8},{8,9},{9,10},{10,1... | collective-permute-start | bytes 307208 | tf_op jit(solution)/shard_map/ppermute | solution.py:23
  60.7 3.2 %collective-permute-start.10 = (f32[2,2,50,1,128]{4,3,0,2,1:T(1,128)S(1)}, f32[2,2,50,1,128]{4,3,0,2,1:T(1,128)S(1)}, u32[]{:S(2)}, u32[]{:S(2)}) collective-permute-start(f32[2,2,50,1,128]{4,3,0,2,1:T(1,128)S(1)} %get-tuple-element.180), channel_id=1, source_target_pairs={{1,0},{2,1},{3,2},{4,3},{5,4},{6,5},{7,6},{8,7},{9,8},{10,9},{11,1... | collective-permute-start | bytes 307208 | tf_op jit(solution)/shard_map/ppermute | solution.py:24
  60.9 7.0 %collective-permute-start.11 = (f32[2,2,50,1,128]{4,3,0,2,1:T(1,128)S(1)}, f32[2,2,50,1,128]{4,3,0,2,1:T(1,128)S(1)}, u32[]{:S(2)}, u32[]{:S(2)}) collective-permute-start(f32[2,2,50,1,128]{4,3,0,2,1:T(1,128)S(1)} %get-tuple-element.181), channel_id=1, source_target_pairs={{0,1},{1,2},{2,3},{3,4},{4,5},{5,6},{6,7},{7,8},{8,9},{9,10},{10,1... | collective-permute-start | bytes 307208 | tf_op jit(solution)/shard_map/ppermute | solution.py:23
  69.2 3.2 %collective-permute-start.12 = (f32[2,2,50,1,128]{4,3,0,2,1:T(1,128)S(1)}, f32[2,2,50,1,128]{4,3,0,2,1:T(1,128)S(1)}, u32[]{:S(2)}, u32[]{:S(2)}) collective-permute-start(f32[2,2,50,1,128]{4,3,0,2,1:T(1,128)S(1)} %get-tuple-element.176), channel_id=1, source_target_pairs={{1,0},{2,1},{3,2},{4,3},{5,4},{6,5},{7,6},{8,7},{9,8},{10,9},{11,1... | collective-permute-start | bytes 307208 | tf_op jit(solution)/shard_map/ppermute | solution.py:24
  70.0 6.8 %collective-permute-start.13 = (f32[2,2,50,1,128]{4,3,0,2,1:T(1,128)S(1)}, f32[2,2,50,1,128]{4,3,0,2,1:T(1,128)S(1)}, u32[]{:S(2)}, u32[]{:S(2)}) collective-permute-start(f32[2,2,50,1,128]{4,3,0,2,1:T(1,128)S(1)} %get-tuple-element.177), channel_id=1, source_target_pairs={{0,1},{1,2},{2,3},{3,4},{4,5},{5,6},{6,7},{7,8},{8,9},{9,10},{10,1... | collective-permute-start | bytes 307208 | tf_op jit(solution)/shard_map/ppermute | solution.py:23
  78.1 1.0 copy-start.10
  79.1 0.7 copy-start.7
  79.1 0.7 copy-start.8
  80.0 102.7 %copy-start.1 = (f32[2,2,50,16,128]{4,3,2,1,0:T(8,128)}, f32[2,2,50,16,128]{4,3,2,1,0:T(8,128)S(1)}, u32[]{:S(2)}) copy-start(f32[2,2,50,16,128]{4,3,2,1,0:T(8,128)S(1)} %fusion.142) | copy-start | bytes 4915204
  180.5 2.2 %copy-start.4 = (f32[50,16,128]{2,1,0:T(8,128)S(1)}, f32[50,16,128]{2,1,0:T(8,128)}, u32[]{:S(2)}) copy-start(f32[50,16,128]{2,1,0:T(8,128)} %param.26) | copy-start | bytes 1228804
Sparse Core Ops, SparseCore 0:
  79.2 101.2 all-gather.2
